TPU v7x, 256 devices: a whole 4x4x8 slice. The times are simulated.
256 devices in a mesh: expert: 16 (over z, core), tensor: 16 (over y, x).
Axes of the slice: x: 4, y: 4, z: 8, core: 2. Of those that a mesh axis runs over, the one named last changes fastest.
Arguments:
- residual_in: bfloat16 [22528, 1024], P(('expert', 'tensor')), may hold values from -6 to 6
- attn_heads: bfloat16 [1024, 22528], P('tensor', 'expert'), may hold values from -6 to 6
- out_proj: bfloat16 [1024, 1024], P('tensor'), may hold values from -0.1875 to 0.1875
- gain_first: float32 [1024], replicated, may hold values from 0.25 to 1.75
- router_weight: float32 [1024, 16], replicated, may hold values from -0.046875 to 0.046875
- routes: int32 [22528, 2], P(('expert', 'tensor')), may hold values from 0 to 15, all different within a row; in each aligned block of 88 rows (0 to 87, 88 to 175, ...) at most 22 rows name the same one
- w_gate: bfloat16 [16, 2816, 1024], P('expert', 'tensor'), may hold values from -0.1875 to 0.1875
- w_upward: bfloat16 [16, 2816, 1024], P('expert', 'tensor'), may hold values from -0.1875 to 0.1875
- w_downward: bfloat16 [16, 2816, 1024], P('expert', 'tensor'), may hold values from -0.21875 to 0.21875
- gain_second: float32 [1024], replicated, may hold values from 0.25 to 1.75
Outputs:
- residual_out: bfloat16 [22528, 1024], P(('expert', 'tensor'))
- next_normed: bfloat16 [22528, 1024], P(('expert', 'tensor'))
Inputs may be any that keep to these rules, and one draw needn't show every extreme that they name: `routes`: each row names two different experts; among the rows of one device no expert is named more than 22 times, and some expert reaches 22.
All inputs are finite; a program needn't handle non-finite values.
Results may differ from a plain program's by a relative error of at most 0.012.
Values may be sent and summed in bfloat16 or wider, within the bound.
No kernel may reach another device: no remote copies, remote signals or barrier semaphores. Data moves between devices by JAX's collectives and lax.ppermute only.
A program may use at most 128 MiB of HBM per device.

v0:
```python
import math
import jax
import jax.numpy as jnp
from jax import lax
from jax.sharding import Mesh
from jax.sharding import PartitionSpec as P

ROWS_AXES = ("expert", "ty", "tx")
TENSOR_AXES = ("ty", "tx")


def rms_scale(values, gain):
    wide = values.astype(jnp.float32)
    scale = lax.rsqrt(jnp.mean(wide * wide, axis=-1, keepdims=True) + 1e-06)
    return (wide * scale * gain).astype(jnp.bfloat16)


def expert_block(inputs, gate_rows, up_rows, down_rows):
    gate_part = lax.dot_general(
        inputs, gate_rows, (((1,), (1,)), ((), ())), preferred_element_type=jnp.float32
    )
    up_part = lax.dot_general(
        inputs, up_rows, (((1,), (1,)), ((), ())), preferred_element_type=jnp.float32
    )
    hid = (jax.nn.gelu(gate_part, approximate=True) * up_part).astype(jnp.bfloat16)
    return jnp.dot(hid, down_rows, preferred_element_type=jnp.float32)


def per_device(
    residual_in,
    attn_heads,
    out_proj,
    gain_first,
    router_weight,
    routes,
    w_gate,
    w_upward,
    w_downward,
    gain_second,
):
    row_count = residual_in.shape[0]
    width = residual_in.shape[1]
    n_expert = lax.axis_size("expert")
    capacity = 4 * row_count // n_expert
    core = lax.axis_index("expert") % 2
    half = width // 2
    my_cols = lax.dynamic_slice_in_dim(out_proj, core * half, half, axis=1)
    my_half = lax.all_gather(my_cols, TENSOR_AXES, axis=0, tiled=True)
    other_half = lax.ppermute(my_half, "expert", [(i, i ^ 1) for i in range(n_expert)])
    own_heads = lax.all_to_all(attn_heads, TENSOR_AXES, 1, 0, tiled=True)
    contract = (((0,), (0,)), ((), ()))
    proj_mine = lax.dot_general(own_heads, my_half, contract, preferred_element_type=jnp.float32)
    proj_other = lax.dot_general(
        own_heads, other_half, contract, preferred_element_type=jnp.float32
    )
    projected = jnp.where(
        core == 0,
        jnp.concatenate([proj_mine, proj_other], axis=1),
        jnp.concatenate([proj_other, proj_mine], axis=1),
    )
    stacked = jnp.concatenate([w_gate, w_upward, w_downward], axis=0)
    n_tx = lax.axis_size("tx")
    pieces = [stacked]
    for shift in range(1, n_tx):
        pieces.append(lax.ppermute(stacked, "tx", [(i, (i + shift) % n_tx) for i in range(n_tx)]))
    hidden_one = (residual_in.astype(jnp.float32) + projected).astype(jnp.bfloat16)
    normed = rms_scale(hidden_one, gain_first)
    logits = jnp.dot(normed.astype(jnp.float32), router_weight, precision=lax.Precision.HIGHEST)
    router_probs = jax.nn.softmax(logits, axis=-1)
    picked = jnp.take_along_axis(router_probs, routes, axis=1)
    gate_weights = picked / jnp.sum(picked, axis=1, keepdims=True)
    flat_ids = routes.reshape(-1)
    expert_iota = jnp.arange(n_expert, dtype=jnp.int32)
    onehot = (flat_ids[:, None] == expert_iota[None, :]).astype(jnp.int32)
    earlier = jnp.cumsum(onehot, axis=0) - onehot
    slot_index = jnp.sum(earlier * onehot, axis=1)
    target = flat_ids * capacity + slot_index
    slot_iota = jnp.arange(n_expert * capacity, dtype=jnp.int32)
    placing = (slot_iota[:, None] == target[None, :]).astype(jnp.bfloat16)
    repeated = jnp.repeat(normed, 2, axis=0)
    send_slots = jnp.dot(placing, repeated, preferred_element_type=jnp.float32).astype(jnp.bfloat16)
    send_slots = send_slots.reshape(n_expert, capacity, width)
    send_slots, *pieces = lax.optimization_barrier((send_slots, *pieces))
    weights = jnp.concatenate(pieces, axis=1)
    gate_rows, up_rows, down_rows = (weights[0], weights[1], weights[2])
    received = lax.all_to_all(send_slots, "expert", split_axis=0, concat_axis=0, tiled=True)
    slot_total = n_expert * capacity
    rows_in = received.reshape(slot_total, width)
    all_rows = lax.all_gather(rows_in, "ty", axis=0, tiled=True)
    expert_sum = lax.psum_scatter(
        expert_block(all_rows, gate_rows, up_rows, down_rows).astype(jnp.bfloat16),
        "ty",
        scatter_dimension=0,
        tiled=True,
    )
    expert_out = expert_sum.reshape(n_expert, capacity, width)
    returned = lax.all_to_all(expert_out, "expert", split_axis=0, concat_axis=0, tiled=True)
    returned = returned.reshape(slot_total, width)
    per_route = lax.dot_general(
        placing, returned, (((0,), (0,)), ((), ())), preferred_element_type=jnp.float32
    )
    per_route = per_route.reshape(row_count, 2, width)
    mixed = jnp.sum(gate_weights[:, :, None] * per_route, axis=1)
    residual_out = (hidden_one.astype(jnp.float32) + mixed).astype(jnp.bfloat16)
    next_normed = rms_scale(residual_out, gain_second)
    return (residual_out, next_normed)


def split_tensor(n):
    inner = int(math.isqrt(n))
    while n % inner:
        inner -= 1
    return (n // inner, inner)


def solution(mesh):
    n_expert = mesh.shape["expert"]
    n_ty, n_tx = split_tensor(mesh.shape["tensor"])
    grid = Mesh(mesh.devices.reshape(n_expert, n_ty, n_tx), ROWS_AXES)
    rows = P(ROWS_AXES, None)
    placed = (
        rows,
        P(TENSOR_AXES, "expert"),
        P(TENSOR_AXES, None),
        P(),
        P(),
        rows,
        P("expert", TENSOR_AXES, None),
        P("expert", TENSOR_AXES, None),
        P("expert", TENSOR_AXES, None),
        P(),
    )
    return jax.shard_map(
        per_device, mesh=grid, in_specs=placed, out_specs=(rows, rows), check_vma=False
    )
```

profile of v0, /device:TPU:1, one launch (start us, length us, event | category | flops | bytes accessed | tf_op | source)
XLA Modules:
  0.0 260.6 jit_solution(8388557563514807960)
XLA Ops:
  7.2 0.0 copy-start
  7.2 0.0 all-gather.3.cloned.1.call-start
  7.3 0.8 copy-done
  8.1 0.6 constant_dynamic-slice_fusion
  8.7 0.0 all-gather.3.cloned.1.call-update
  8.7 1.0 constant_dynamic-update-slice_fusion.2
  9.7 1.0 constant_dynamic-update-slice_fusion.1
  10.8 1.0 constant_dynamic-update-slice_fusion
  11.8 2.1 collective-permute-start.1
  13.9 2.5 collective-permute-start.2
  16.3 1.2 collective-permute-start.3
  17.5 1.4 all_to_all.20
  18.9 0.8 copy.23
  19.7 4.3 %all-to-all-start = ((bf16[64,16,88]{2,0,1:T(8,128)(2,1)}), bf16[64,16,88]{2,0,1:T(8,128)(2,1)S(1)}, u32[]{:S(2)}, u32[]{:S(2)}) async-start(bf16[64,16,88]{2,0,1:T(8,128)(2,1)} %copy.23), calls=%async_computation | async-start | bytes 524288 | tf_op jit(solution)/shard_map/all_to_all | solution.py:50
  24.0 0.0 all-gather.5.cloned.1.call-start
  24.1 0.8 copy.26
  24.9 0.1 reshape.112
  25.0 66.8 %all-gather.3.cloned.1.call-done = bf16[1024,512]{1,0:T(8,128)(2,1)} async-done(((bf16[64,512]{1,0:T(8,128)(2,1)}), bf16[1024,512]{1,0:T(8,128)(2,1)}) %all-gather.3.cloned.1.call-update) | async-done | bytes 1048592 | tf_op jit(solution)/shard_map/all_gather | solution.py:48
  91.8 2.4 collective-permute-start
  94.2 0.6 reduce-window.6
  94.8 0.2 slice_reduce_fusion
  95.0 0.1 bitcast_bitcast_fusion
  95.2 0.0 all-to-all-done
  95.2 1.6 convolution_bitcast_fusion.1
  96.7 0.0 collective-permute-done
  96.7 0.3 convolution_bitcast_fusion
  97.1 0.2 fusion.14
  97.3 0.1 fusion.16
  97.4 0.2 broadcast_in_dim.7
  97.6 0.1 reshape.115
  97.7 0.3 convolution_convert_fusion.1
  98.1 0.2 reshape.116
  98.3 0.0 collective-permute-done.1
  98.3 0.0 collective-permute-done.2
  98.3 0.0 collective-permute-done.3
  98.3 30.0 %all_to_all.29 = bf16[16,22,1024]{2,1,0:T(8,128)(2,1)S(1)} all-to-all(bf16[16,22,1024]{2,1,0:T(8,128)(2,1)S(1)} %reshape.116), channel_id=1, replica_groups=mesh['expert'=16,'ty'=4,'tx'=4] {'expert'}, dimensions={0} | all-to-all | bytes 1441792 | tf_op jit(solution)/shard_map/all_to_all | solution.py:86
  128.3 1.1 reshape.117
  129.4 0.0 all-gather.5.cloned.1.call-update
  129.4 0.2 reduce-scatter.2.cloned.1.call-start
  129.6 1.1 constant_dynamic-update-slice_fusion.6
  130.7 2.3 constant_dynamic-update-slice_fusion.5
  133.0 2.3 constant_dynamic-update-slice_fusion.4
  135.3 2.4 constant_dynamic-update-slice_fusion.3
  137.6 26.3 %all-gather.5.cloned.1.call-done = bf16[1408,1024]{1,0:T(8,128)(2,1)} async-done(((bf16[352,1024]{1,0:T(8,128)(2,1)}), bf16[1408,1024]{1,0:T(8,128)(2,1)}) %all-gather.5.cloned.1.call-update) | async-done | bytes 2883600 | tf_op jit(solution)/shard_map/all_gather | solution.py:89
  164.0 6.6 %fusion.9 = f32[1408,704]{0,1:T(8,128)} fusion(bf16[1408,1024]{1,0:T(8,128)(2,1)} %all-gather.5.cloned.1.call-done, bf16[3,704,1024]{2,1,0:T(8,128)(2,1)} %constant_dynamic-update-slice_fusion.3), kind=kOutput, calls=%fused_computation.15 | convolution fusion | flops 2030043136 | bytes 8290304 | tf_op jit(solution)/shard_map/dot_general | solution.py:19
  170.5 10.3 %convolution_convert_fusion = bf16[1408,1024]{1,0:T(8,128)(2,1)} fusion(bf16[3,704,1024]{2,1,0:T(8,128)(2,1)} %constant_dynamic-update-slice_fusion.3, f32[1408,704]{0,1:T(8,128)} %fusion.9, bf16[1408,1024]{1,0:T(8,128)(2,1)} %all-gather.5.cloned.1.call-done), kind=kOutput, calls=%fused_computation.11 | convolution fusion | flops 4071440384 | bytes 12615680 | tf_op jit(solution)/shard_map/dot_general | solution.py:26
  180.8 0.0 reduce-scatter.2.cloned.1.call-update
  180.9 39.1 %reduce-scatter.2.cloned.1.call-done = bf16[352,1024]{1,0:T(8,128)(2,1)} async-done(((bf16[1408,1024]{1,0:T(8,128)(2,1)}), bf16[352,1024]{1,0:T(8,128)(2,1)}) %reduce-scatter.2.cloned.1.call-update) | async-done | bytes 720912 | tf_op jit(solution)/shard_map/reduce_scatter | solution.py:90
  220.0 2.1 reshape.118
  222.1 7.8 %all-to-all-start.2 = ((bf16[16,22,1024]{2,1,0:T(8,128)(2,1)}), bf16[16,22,1024]{2,1,0:T(8,128)(2,1)S(1)}, u32[]{:S(2)}, u32[]{:S(2)}) async-start(bf16[16,22,1024]{2,1,0:T(8,128)(2,1)} %reshape.118), calls=%async_computation.3 | async-start | bytes 1572864 | tf_op jit(solution)/shard_map/all_to_all | solution.py:97
  229.8 0.1 copy.24
  229.9 0.1 reshape.121
  230.1 0.1 iota_compare_fusion.2
  230.2 0.1 eq.63
  230.3 0.3 fusion.33
  230.6 0.0 copy-start.6
  230.6 2.3 gather_fusion
  232.9 0.1 reshape.124
  233.0 0.1 copy.25
  233.2 19.4 %all-to-all-done.2 = bf16[16,22,1024]{2,1,0:T(8,128)(2,1)S(1)} async-done(((bf16[16,22,1024]{2,1,0:T(8,128)(2,1)}), bf16[16,22,1024]{2,1,0:T(8,128)(2,1)S(1)}, u32[]{:S(2)}, u32[]{:S(2)}) %all-to-all-start.2) | async-done | bytes 720928 | tf_op jit(solution)/shard_map/all_to_all | solution.py:97
  252.5 0.2 reshape.132
  252.8 0.4 fusion.10
  253.1 0.2 fusion.11
  253.3 0.8 fusion.13
  (24 shorter events, 0.2 us)
Async XLA Ops:
  7.2 0.9 copy-start
  7.2 89.9 %copy-start.2 = (bf16[88,1024]{1,0:T(8,128)(2,1)S(1)}, bf16[88,1024]{1,0:T(8,128)(2,1)}, u32[]{:S(2)}) copy-start(bf16[88,1024]{1,0:T(8,128)(2,1)} %param.10) | copy-start | bytes 540676
  7.2 90.1 %copy-start.5 = (f32[1024]{0:T(1024)S(1)}, f32[1024]{0:T(1024)}, u32[]{:S(2)}) copy-start(f32[1024]{0:T(1024)} %param.13) | copy-start | bytes 12292
  7.2 84.6 %all-gather.3.cloned.1.call-start = ((), (), s32[]{:S(2)}) async-start(), calls=%async_computation.4 | async-start | bytes 1114112 | tf_op jit(solution)/shard_map/all_gather | solution.py:48
  11.8 86.5 %collective-permute-start.1 = (bf16[3,176,1024]{2,1,0:T(8,128)(2,1)S(1)}, bf16[3,176,1024]{2,1,0:T(8,128)(2,1)}, u32[]{:S(2)}, u32[]{:S(2)}) collective-permute-start(bf16[3,176,1024]{2,1,0:T(8,128)(2,1)S(1)} %constant_dynamic-update-slice_fusion), channel_id=1, source_target_pairs={{0,1},{1,2},{2,3},{3,0},{4,5},{5,6},{6,7},{7,4},{8,9},{9,10},{10,1... | collective-permute-start | bytes 3244040 | tf_op jit(solution)/shard_map/ppermute | solution.py:65
  13.9 84.4 %collective-permute-start.2 = (bf16[3,176,1024]{2,1,0:T(8,128)(2,1)S(1)}, bf16[3,176,1024]{2,1,0:T(8,128)(2,1)}, u32[]{:S(2)}, u32[]{:S(2)}) collective-permute-start(bf16[3,176,1024]{2,1,0:T(8,128)(2,1)S(1)} %constant_dynamic-update-slice_fusion), channel_id=1, source_target_pairs={{0,2},{1,3},{2,0},{3,1},{4,6},{5,7},{6,4},{7,5},{8,10},{9,11},{10,... | collective-permute-start | bytes 3244040 | tf_op jit(solution)/shard_map/ppermute | solution.py:65
  16.3 82.0 %collective-permute-start.3 = (bf16[3,176,1024]{2,1,0:T(8,128)(2,1)S(1)}, bf16[3,176,1024]{2,1,0:T(8,128)(2,1)}, u32[]{:S(2)}, u32[]{:S(2)}) collective-permute-start(bf16[3,176,1024]{2,1,0:T(8,128)(2,1)S(1)} %constant_dynamic-update-slice_fusion), channel_id=1, source_target_pairs={{0,3},{1,0},{2,1},{3,2},{4,7},{5,4},{6,5},{7,6},{8,11},{9,8},{10,9... | collective-permute-start | bytes 3244040 | tf_op jit(solution)/shard_map/ppermute | solution.py:65
  19.7 75.5 %all-to-all-start = ((bf16[64,16,88]{2,0,1:T(8,128)(2,1)}), bf16[64,16,88]{2,0,1:T(8,128)(2,1)S(1)}, u32[]{:S(2)}, u32[]{:S(2)}) async-start(bf16[64,16,88]{2,0,1:T(8,128)(2,1)} %copy.23), calls=%async_computation | async-start | bytes 524288 | tf_op jit(solution)/shard_map/all_to_all | solution.py:50
  24.0 140.0 %all-gather.5.cloned.1.call-start = ((), (), s32[]{:S(2)}) async-start(), calls=%async_computation.5 | async-start | bytes 3604480 | tf_op jit(solution)/shard_map/all_gather | solution.py:89
  91.8 4.9 %collective-permute-start = (bf16[1024,512]{1,0:T(8,128)(2,1)}, bf16[1024,512]{1,0:T(8,128)(2,1)S(1)}, u32[]{:S(2)}, u32[]{:S(2)}) collective-permute-start(bf16[1024,512]{1,0:T(8,128)(2,1)} %all-gather.3.cloned.1.call-done), channel_id=1, source_target_pairs={{0,16},{16,0},{32,48},{48,32},{64,80},{80,64},{96,112},{112,96},{1... | collective-permute-start | bytes 3145736 | tf_op jit(solution)/shard_map/ppermute | solution.py:49
  129.4 90.6 %reduce-scatter.2.cloned.1.call-start = ((), (), s32[]{:S(2)}) async-start(), calls=%async_computation.6 | async-start | bytes 3604480 | tf_op jit(solution)/shard_map/reduce_scatter | solution.py:90
  180.8 49.0 %copy-start.4 = (s32[88,2]{0,1:T(2,128)S(1)}, s32[88,2]{0,1:T(2,128)}, u32[]{:S(2)}) copy-start(s32[88,2]{0,1:T(2,128)} %param.15) | copy-start | bytes 2116
  180.8 49.5 %copy-start.3 = (f32[1024,16]{0,1:T(8,128)S(1)}, f32[1024,16]{0,1:T(8,128)}, u32[]{:S(2)}) copy-start(f32[1024,16]{0,1:T(8,128)} %param.14) | copy-start | bytes 196612
  222.1 30.5 %all-to-all-start.2 = ((bf16[16,22,1024]{2,1,0:T(8,128)(2,1)}), bf16[16,22,1024]{2,1,0:T(8,128)(2,1)S(1)}, u32[]{:S(2)}, u32[]{:S(2)}) async-start(bf16[16,22,1024]{2,1,0:T(8,128)(2,1)} %reshape.118), calls=%async_computation.3 | async-start | bytes 1572864 | tf_op jit(solution)/shard_map/all_to_all | solution.py:97
  230.6 22.7 %copy-start.6 = (f32[1024]{0:T(1024)S(1)}, f32[1024]{0:T(1024)}, u32[]{:S(2)}) copy-start(f32[1024]{0:T(1024)} %param.19) | copy-start | bytes 12292
  253.3 0.8 copy-start.1
Sparse Core Ops, SparseCore 0:
  11.0 80.7 all-gather.2
  129.5 34.4 all-gather.4
  181.0 38.9 reduce-scatter.1
where the time goes:
time: 261 us
  waiting for transfers between devices  152 us (58%)
  blocking collectives  30 us (11%)
  local copies, waits for them, and re-layouts  22.5 us (9%)
  starting transfers between devices  20.5 us (8%)
  matrix products  19.7 us (8%)
  between operations  14 us (5%)
    all_gather x1, waiting for transfers between devices, per_device(): my_half = lax.all_gather(my_cols, TENSOR_AXES, axis=0, tiled=True)  66.8 us
    reduce_scatter x1, waiting for transfers between devices, per_device(): lax.psum_scatter(expert_block(all_rows, gate_rows, up_rows, down_rows).as...  39.1 us
    all_to_all x1, blocking collectives, per_device(): lax.all_to_all(send_slots, 'expert', split_axis=0, concat_axis=0, tiled=T...  30 us
    all_gather x1, waiting for transfers between devices, per_device(): all_rows = lax.all_gather(rows_in, 'ty', axis=0, tiled=True)  26.3 us
    all_to_all x1, waiting for transfers between devices, per_device(): lax.all_to_all(expert_out, 'expert', split_axis=0, concat_axis=0, tiled=T...  19.4 us
    dot_general x1, matrix products, expert_block(): return jnp.dot(hid, down_rows, preferred_element_type=jnp.float32)  10.3 us
    unnamed x20, local copies, waits for them, and re-layouts  9.27 us
    all_to_all x1, starting transfers between devices, per_device(): lax.all_to_all(expert_out, 'expert', split_axis=0, concat_axis=0, tiled=T...  7.76 us
  transfers between devices with their start and end apart: 9, of which 4 were waited for; matrix products, arithmetic and copies ran while one was open for 8% of the time, Pallas kernels for 0%

commit v1 on v0

--- a/solution.py
+++ b/solution.py
@@ -7,6 +7,9 @@
 
 ROWS_AXES = ("expert", "ty", "tx")
 TENSOR_AXES = ("ty", "tx")
+state_sample = lambda m, mesh_dim: jnp.concatenate(
+    lax.all_to_all(jnp.stack([m] * lax.axis_size(mesh_dim), axis=0), mesh_dim, 0, 0), axis=0
+)
 
 
 def rms_scale(values, gain):
@@ -45,7 +48,7 @@
     core = lax.axis_index("expert") % 2
     half = width // 2
     my_cols = lax.dynamic_slice_in_dim(out_proj, core * half, half, axis=1)
-    my_half = lax.all_gather(my_cols, TENSOR_AXES, axis=0, tiled=True)
+    my_half = state_sample(my_cols, TENSOR_AXES)
     other_half = lax.ppermute(my_half, "expert", [(i, i ^ 1) for i in range(n_expert)])
     own_heads = lax.all_to_all(attn_heads, TENSOR_AXES, 1, 0, tiled=True)
     contract = (((0,), (0,)), ((), ()))

time: 261 us -> 250 us (0.958)
  waiting for transfers between devices: 152 us -> 114 us
  starting transfers between devices: 20.5 us -> 47 us
  local copies, waits for them, and re-layouts: 22.5 us -> 19.4 us
  blocking collectives: 30 us -> 32.9 us
    all_gather x1 -> x0, waiting for transfers between devices: 66.8 us -> none  [per_device(): my_half = lax.all_gather(my_cols, TENSOR_AXES, axis=0, tiled=True)]
    all_to_all x1, waiting for transfers between devices: 0.01 us -> 22.2 us  [per_device(): own_heads = lax.all_to_all(attn_heads, TENSOR_AXES, 1, 0, tiled=True)]
    ppermute x1, starting transfers between devices: 2.44 us -> 22.1 us  [per_device(): lax.ppermute(my_half, 'expert', [(i, i ^ 1) for i in range(n_expert)])]
    all_to_all x0 -> x1, waiting for transfers between devices: none -> 8.37 us  [lax.all_to_all(jnp.stack([m] * lax.axis_size(mesh_dim), axis=0), mesh_dim...]
    all_to_all x0 -> x1, starting transfers between devices: none -> 7.7 us  [lax.all_to_all(jnp.stack([m] * lax.axis_size(mesh_dim), axis=0), mesh_dim...]
    all_to_all x1, blocking collectives: 30 us -> 32.9 us  [per_device(): lax.all_to_all(send_slots, 'expert', split_axis=0, concat_axis=0, tiled=T...]
    unnamed x20 -> x26, local copies, waits for them, and re-layouts: 9.27 us -> 7.67 us
  transfers between devices with their start and end apart: 9 -> 9, of which waited for: 4 -> 5; matrix products, arithmetic and copies ran while one was open for 8% -> 7% of each run, Pallas kernels for 0% -> 0%
where the time goes in v1:
time: 250 us
  waiting for transfers between devices  114 us (46%)
  starting transfers between devices  47 us (19%)
  blocking collectives  32.9 us (13%)
  matrix products  19.7 us (8%)
  local copies, waits for them, and re-layouts  19.4 us (8%)
  between operations  14.4 us (6%)
    reduce_scatter x1, waiting for transfers between devices, per_device(): lax.psum_scatter(expert_block(all_rows, gate_rows, up_rows, down_rows).as...  39.1 us
    all_to_all x1, blocking collectives, per_device(): lax.all_to_all(send_slots, 'expert', split_axis=0, concat_axis=0, tiled=T...  32.9 us
    all_gather x1, waiting for transfers between devices, per_device(): all_rows = lax.all_gather(rows_in, 'ty', axis=0, tiled=True)  25 us
    all_to_all x1, waiting for transfers between devices, per_device(): own_heads = lax.all_to_all(attn_heads, TENSOR_AXES, 1, 0, tiled=True)  22.2 us
    ppermute x1, starting transfers between devices, per_device(): lax.ppermute(my_half, 'expert', [(i, i ^ 1) for i in range(n_expert)])  22.1 us
    all_to_all x1, waiting for transfers between devices, per_device(): lax.all_to_all(expert_out, 'expert', split_axis=0, concat_axis=0, tiled=T...  19.4 us
    dot_general x1, matrix products, expert_block(): return jnp.dot(hid, down_rows, preferred_element_type=jnp.float32)  10.3 us
    all_to_all x1, waiting for transfers between devices, lax.all_to_all(jnp.stack([m] * lax.axis_size(mesh_dim), axis=0), mesh_dim...  8.37 us
  transfers between devices with their start and end apart: 9, of which 5 were waited for; matrix products, arithmetic and copies ran while one was open for 7% of the time, Pallas kernels for 0%

profile of v1, /device:TPU:1, one launch (start us, length us, event | category | flops | bytes accessed | tf_op | source)
XLA Modules:
  0.0 249.7 jit_solution(69897519057126350)
XLA Ops:
  7.2 0.0 copy-start
  7.2 0.8 copy-done
  8.1 1.1 stack.2
  9.2 7.7 %all-to-all-start = ((bf16[16,64,512]{2,1,0:T(8,128)(2,1)}), bf16[16,64,512]{2,1,0:T(8,128)(2,1)S(1)}, u32[]{:S(2)}, u32[]{:S(2)}) async-start(bf16[16,64,512]{2,1,0:T(8,128)(2,1)} %stack.2), calls=%async_computation | async-start | bytes 2097152 | tf_op jit(solution)/shard_map/all_to_all | solution.py:11
  16.9 0.0 copy-start.8
  16.9 1.0 constant_dynamic-update-slice_fusion.2
  18.0 1.4 collective-permute-start.1
  19.4 2.4 collective-permute-start.2
  21.8 1.2 collective-permute-start.3
  23.0 0.5 all_to_all.24
  23.5 0.8 copy.23
  24.3 0.0 copy-done.7
  24.3 0.1 copy.26
  24.4 0.1 reshape.118
  24.6 8.4 %all-to-all-done = bf16[16,64,512]{2,1,0:T(8,128)(2,1)S(1)} async-done(((bf16[16,64,512]{2,1,0:T(8,128)(2,1)}), bf16[16,64,512]{2,1,0:T(8,128)(2,1)S(1)}, u32[]{:S(2)}, u32[]{:S(2)}) %all-to-all-start) | async-done | bytes 1048608 | tf_op jit(solution)/shard_map/all_to_all | solution.py:11
  32.9 4.2 %all-to-all-start.1 = ((bf16[64,16,88]{2,0,1:T(8,128)(2,1)}), bf16[64,16,88]{2,0,1:T(8,128)(2,1)S(1)}, u32[]{:S(2)}, u32[]{:S(2)}) async-start(bf16[64,16,88]{2,0,1:T(8,128)(2,1)} %copy.23), calls=%async_computation.1 | async-start | bytes 524288 | tf_op jit(solution)/shard_map/all_to_all | solution.py:53
  37.1 0.0 all-gather.2.cloned.1.call-start
  37.2 22.1 %collective-permute-start = (bf16[1024,512]{1,0:T(8,128)(2,1)S(1)}, bf16[1024,512]{1,0:T(8,128)(2,1)}, u32[]{:S(2)}, u32[]{:S(2)}) collective-permute-start(bf16[1024,512]{1,0:T(8,128)(2,1)S(1)} %bitcast.48), channel_id=1, source_target_pairs={{0,16},{16,0},{32,48},{48,32},{64,80},{80,64},{96,112},{112,96},{1... | collective-permute-start | bytes 3145736 | tf_op jit(solution)/shard_map/ppermute | solution.py:52
  59.3 0.6 reduce-window.6
  59.9 0.2 slice_reduce_fusion
  60.1 0.1 bitcast_bitcast_fusion
  60.2 22.2 %all-to-all-done.1 = bf16[64,16,88]{2,0,1:T(8,128)(2,1)S(1)} async-done(((bf16[64,16,88]{2,0,1:T(8,128)(2,1)}), bf16[64,16,88]{2,0,1:T(8,128)(2,1)S(1)}, u32[]{:S(2)}, u32[]{:S(2)}) %all-to-all-start.1) | async-done | bytes 180256 | tf_op jit(solution)/shard_map/all_to_all | solution.py:53
  82.4 0.3 convolution_bitcast_fusion.1
  82.8 0.0 collective-permute-done
  82.8 1.6 convolution_bitcast_fusion
  84.3 0.2 fusion.14
  84.5 0.1 fusion.16
  84.6 0.2 broadcast_in_dim.7
  84.8 0.1 reshape.121
  85.0 0.3 convolution_convert_fusion.1
  85.3 0.2 reshape.122
  85.6 0.0 collective-permute-done.1
  85.6 0.0 collective-permute-done.2
  85.6 0.0 collective-permute-done.3
  85.6 32.9 %all_to_all.34 = bf16[16,22,1024]{2,1,0:T(8,128)(2,1)S(1)} all-to-all(bf16[16,22,1024]{2,1,0:T(8,128)(2,1)S(1)} %reshape.122), channel_id=1, replica_groups=mesh['expert'=16,'ty'=4,'tx'=4] {'expert'}, dimensions={0} | all-to-all | bytes 1441792 | tf_op jit(solution)/shard_map/all_to_all | solution.py:89
  118.4 1.1 reshape.123
  119.5 0.0 all-gather.2.cloned.1.call-update
  119.5 0.2 reduce-scatter.2.cloned.1.call-start
  119.8 1.1 constant_dynamic-update-slice_fusion.6
  120.8 2.3 constant_dynamic-update-slice_fusion.5
  123.1 2.3 constant_dynamic-update-slice_fusion.4
  125.4 2.4 constant_dynamic-update-slice_fusion.3
  127.8 25.0 %all-gather.2.cloned.1.call-done = bf16[1408,1024]{1,0:T(8,128)(2,1)} async-done(((bf16[352,1024]{1,0:T(8,128)(2,1)}), bf16[1408,1024]{1,0:T(8,128)(2,1)}) %all-gather.2.cloned.1.call-update) | async-done | bytes 2883600 | tf_op jit(solution)/shard_map/all_gather | solution.py:92
  152.7 6.6 %fusion.9 = f32[1408,704]{0,1:T(8,128)} fusion(bf16[1408,1024]{1,0:T(8,128)(2,1)} %all-gather.2.cloned.1.call-done, bf16[3,704,1024]{2,1,0:T(8,128)(2,1)} %constant_dynamic-update-slice_fusion.3), kind=kOutput, calls=%fused_computation.15 | convolution fusion | flops 2030043136 | bytes 8290304 | tf_op jit(solution)/shard_map/dot_general | solution.py:22
  159.3 10.3 %convolution_convert_fusion = bf16[1408,1024]{1,0:T(8,128)(2,1)} fusion(bf16[3,704,1024]{2,1,0:T(8,128)(2,1)} %constant_dynamic-update-slice_fusion.3, f32[1408,704]{0,1:T(8,128)} %fusion.9, bf16[1408,1024]{1,0:T(8,128)(2,1)} %all-gather.2.cloned.1.call-done), kind=kOutput, calls=%fused_computation.11 | convolution fusion | flops 4071440384 | bytes 12615680 | tf_op jit(solution)/shard_map/dot_general | solution.py:29
  169.6 0.0 reduce-scatter.2.cloned.1.call-update
  169.6 39.1 %reduce-scatter.2.cloned.1.call-done = bf16[352,1024]{1,0:T(8,128)(2,1)} async-done(((bf16[1408,1024]{1,0:T(8,128)(2,1)}), bf16[352,1024]{1,0:T(8,128)(2,1)}) %reduce-scatter.2.cloned.1.call-update) | async-done | bytes 720912 | tf_op jit(solution)/shard_map/reduce_scatter | solution.py:93
  208.7 2.1 reshape.124
  210.8 7.8 %all-to-all-start.3 = ((bf16[16,22,1024]{2,1,0:T(8,128)(2,1)}), bf16[16,22,1024]{2,1,0:T(8,128)(2,1)S(1)}, u32[]{:S(2)}, u32[]{:S(2)}) async-start(bf16[16,22,1024]{2,1,0:T(8,128)(2,1)} %reshape.124), calls=%async_computation.4 | async-start | bytes 1572864 | tf_op jit(solution)/shard_map/all_to_all | solution.py:100
  218.6 0.1 copy.24
  218.7 0.1 reshape.127
  218.8 0.1 iota_compare_fusion.2
  218.9 0.1 eq.63
  219.0 0.0 copy-done.6
  219.0 0.3 fusion.34
  219.4 0.0 copy-start.9
  219.4 2.3 gather_fusion
  221.7 0.1 reshape.130
  221.8 0.1 copy.25
  221.9 19.4 %all-to-all-done.3 = bf16[16,22,1024]{2,1,0:T(8,128)(2,1)S(1)} async-done(((bf16[16,22,1024]{2,1,0:T(8,128)(2,1)}), bf16[16,22,1024]{2,1,0:T(8,128)(2,1)S(1)}, u32[]{:S(2)}, u32[]{:S(2)}) %all-to-all-start.3) | async-done | bytes 720928 | tf_op jit(solution)/shard_map/all_to_all | solution.py:100
  241.3 0.2 reshape.139
  241.5 0.4 fusion.10
  241.9 0.1 fusion.11
  242.0 0.8 fusion.13
  (30 shorter events, 0.3 us)
Async XLA Ops:
  7.2 0.9 copy-start
  7.2 10.7 %copy-start.2 = (bf16[1,176,1024]{2,1,0:T(8,128)(2,1)S(1)}, bf16[1,176,1024]{2,1,0:T(8,128)(2,1)}, u32[]{:S(2)}) copy-start(bf16[1,176,1024]{2,1,0:T(8,128)(2,1)} %param.17) | copy-start | bytes 1081348
  7.2 10.8 %copy-start.3 = (bf16[1,176,1024]{2,1,0:T(8,128)(2,1)S(1)}, bf16[1,176,1024]{2,1,0:T(8,128)(2,1)}, u32[]{:S(2)}) copy-start(bf16[1,176,1024]{2,1,0:T(8,128)(2,1)} %param.18) | copy-start | bytes 1081348
  7.2 15.8 %copy-start.4 = (bf16[64,1408]{1,0:T(8,128)(2,1)S(1)}, bf16[64,1408]{1,0:T(8,128)(2,1)}, u32[]{:S(2)}) copy-start(bf16[64,1408]{1,0:T(8,128)(2,1)} %param.11) | copy-start | bytes 540676
  7.2 17.1 %copy-start.7 = (s32[88,2]{0,1:T(2,128)S(1)}, s32[88,2]{0,1:T(2,128)}, u32[]{:S(2)}) copy-start(s32[88,2]{0,1:T(2,128)} %param.15) | copy-start | bytes 2116
  9.2 75.2 %copy-start.5 = (bf16[88,1024]{1,0:T(8,128)(2,1)S(1)}, bf16[88,1024]{1,0:T(8,128)(2,1)}, u32[]{:S(2)}) copy-start(bf16[88,1024]{1,0:T(8,128)(2,1)} %param.10) | copy-start | bytes 540676
  9.2 23.8 %all-to-all-start = ((bf16[16,64,512]{2,1,0:T(8,128)(2,1)}), bf16[16,64,512]{2,1,0:T(8,128)(2,1)S(1)}, u32[]{:S(2)}, u32[]{:S(2)}) async-start(bf16[16,64,512]{2,1,0:T(8,128)(2,1)} %stack.2), calls=%async_computation | async-start | bytes 2097152 | tf_op jit(solution)/shard_map/all_to_all | solution.py:11
  16.9 67.6 %copy-start.8 = (f32[1024]{0:T(1024)S(1)}, f32[1024]{0:T(1024)}, u32[]{:S(2)}) copy-start(f32[1024]{0:T(1024)} %param.13) | copy-start | bytes 12292
  18.0 67.5 %collective-permute-start.1 = (bf16[3,176,1024]{2,1,0:T(8,128)(2,1)S(1)}, bf16[3,176,1024]{2,1,0:T(8,128)(2,1)}, u32[]{:S(2)}, u32[]{:S(2)}) collective-permute-start(bf16[3,176,1024]{2,1,0:T(8,128)(2,1)S(1)} %constant_dynamic-update-slice_fusion), channel_id=1, source_target_pairs={{0,1},{1,2},{2,3},{3,0},{4,5},{5,6},{6,7},{7,4},{8,9},{9,10},{10,1... | collective-permute-start | bytes 3244040 | tf_op jit(solution)/shard_map/ppermute | solution.py:68
  19.4 66.1 %collective-permute-start.2 = (bf16[3,176,1024]{2,1,0:T(8,128)(2,1)S(1)}, bf16[3,176,1024]{2,1,0:T(8,128)(2,1)}, u32[]{:S(2)}, u32[]{:S(2)}) collective-permute-start(bf16[3,176,1024]{2,1,0:T(8,128)(2,1)S(1)} %constant_dynamic-update-slice_fusion), channel_id=1, source_target_pairs={{0,2},{1,3},{2,0},{3,1},{4,6},{5,7},{6,4},{7,5},{8,10},{9,11},{10,... | collective-permute-start | bytes 3244040 | tf_op jit(solution)/shard_map/ppermute | solution.py:68
  21.8 63.7 %collective-permute-start.3 = (bf16[3,176,1024]{2,1,0:T(8,128)(2,1)S(1)}, bf16[3,176,1024]{2,1,0:T(8,128)(2,1)}, u32[]{:S(2)}, u32[]{:S(2)}) collective-permute-start(bf16[3,176,1024]{2,1,0:T(8,128)(2,1)S(1)} %constant_dynamic-update-slice_fusion), channel_id=1, source_target_pairs={{0,3},{1,0},{2,1},{3,2},{4,7},{5,4},{6,5},{7,6},{8,11},{9,8},{10,9... | collective-permute-start | bytes 3244040 | tf_op jit(solution)/shard_map/ppermute | solution.py:68
  32.9 49.5 %all-to-all-start.1 = ((bf16[64,16,88]{2,0,1:T(8,128)(2,1)}), bf16[64,16,88]{2,0,1:T(8,128)(2,1)S(1)}, u32[]{:S(2)}, u32[]{:S(2)}) async-start(bf16[64,16,88]{2,0,1:T(8,128)(2,1)} %copy.23), calls=%async_computation.1 | async-start | bytes 524288 | tf_op jit(solution)/shard_map/all_to_all | solution.py:53
  37.1 115.6 %all-gather.2.cloned.1.call-start = ((), (), s32[]{:S(2)}) async-start(), calls=%async_computation.5 | async-start | bytes 3604480 | tf_op jit(solution)/shard_map/all_gather | solution.py:92
  37.2 45.6 %collective-permute-start = (bf16[1024,512]{1,0:T(8,128)(2,1)S(1)}, bf16[1024,512]{1,0:T(8,128)(2,1)}, u32[]{:S(2)}, u32[]{:S(2)}) collective-permute-start(bf16[1024,512]{1,0:T(8,128)(2,1)S(1)} %bitcast.48), channel_id=1, source_target_pairs={{0,16},{16,0},{32,48},{48,32},{64,80},{80,64},{96,112},{112,96},{1... | collective-permute-start | bytes 3145736 | tf_op jit(solution)/shard_map/ppermute | solution.py:52
  119.5 89.2 %reduce-scatter.2.cloned.1.call-start = ((), (), s32[]{:S(2)}) async-start(), calls=%async_computation.6 | async-start | bytes 3604480 | tf_op jit(solution)/shard_map/reduce_scatter | solution.py:93
  169.6 49.5 %copy-start.6 = (f32[1024,16]{0,1:T(8,128)S(1)}, f32[1024,16]{0,1:T(8,128)}, u32[]{:S(2)}) copy-start(f32[1024,16]{0,1:T(8,128)} %param.14) | copy-start | bytes 196612
  210.8 30.5 %all-to-all-start.3 = ((bf16[16,22,1024]{2,1,0:T(8,128)(2,1)}), bf16[16,22,1024]{2,1,0:T(8,128)(2,1)S(1)}, u32[]{:S(2)}, u32[]{:S(2)}) async-start(bf16[16,22,1024]{2,1,0:T(8,128)(2,1)} %reshape.124), calls=%async_computation.4 | async-start | bytes 1572864 | tf_op jit(solution)/shard_map/all_to_all | solution.py:100
  219.4 22.7 %copy-start.9 = (f32[1024]{0:T(1024)S(1)}, f32[1024]{0:T(1024)}, u32[]{:S(2)}) copy-start(f32[1024]{0:T(1024)} %param.19) | copy-start | bytes 12292
  242.0 0.8 copy-start.1
Sparse Core Ops, SparseCore 0:
  119.6 33.0 all-gather.1
  169.7 38.9 reduce-scatter.1
